TPU v7x, 256 devices: a whole 4x4x8 slice. The times are simulated.
256 devices in a mesh: space: 8 (over x_hi, y), species: 32 (over z, x_lo, core).
Axes of the slice: x: 4 (x_hi: 2, x_lo: 2; x = x_hi * 2 + x_lo), y: 4, z: 8, core: 2. Of those that a mesh axis runs over, the one named last changes fastest.
Arguments:
- dust_state: float32 [3, 128, 256, 1024], P(None, 'species', 'space'), may hold values from -4 to 4, as said below
- gas_state: float32 [3, 256, 1024], P(None, 'space'), may hold values from -2 to 2, as said below
- species_bin: int32 [128], P('species'), may hold values from 0 to 127, each once
Outputs:
- dust_out: float32 [3, 128, 256, 1024], P(None, 'species', 'space')
- gas_out: float32 [3, 256, 1024], P(None, 'space')
Inputs may be any that keep to these rules, and one draw needn't show every extreme that they name: `dust_state`: component 0 (densities) lies in 0.5 to 2; the velocities lie within -4 to 4. `gas_state`: component 0 (density) lies in 0.5 to 2; the velocities lie within -2 to 2.
All inputs are finite; a program needn't handle non-finite values.
Results may differ from a plain program's by a relative error of at most 0.0003.
Values sent between devices are 32-bit elements; how exact they have to be, the bound alone decides.
No kernel may reach another device: no remote copies, remote signals or barrier semaphores. Data moves between devices by JAX's collectives and lax.ppermute only.
A program may use at most 64 MiB of HBM per device.

v0:
```python
import jax
import jax.numpy as jnp
from jax import lax
from jax.sharding import PartitionSpec as P

STEPS = 2
courant = 0.25
sound_speed = 1.0
sound_sq = 1.0
stop_floor = 0.003
stop_span = 6.907755


def padded(block, sides, width):
    for axis, dim in sides:
        count = lax.axis_size(axis)
        forward = [(i, i + 1) for i in range(count - 1)]
        forward.append((count - 1, 0))
        backward = [(target, source) for source, target in forward]
        low = lax.ppermute(
            lax.slice_in_dim(block, block.shape[dim] - width, None, axis=dim), axis, forward
        )
        high = lax.ppermute(lax.slice_in_dim(block, 0, width, axis=dim), axis, backward)
        block = jnp.concatenate([low, block, high], axis=dim)
    return block


def window(values, start, length, along):
    return lax.slice_in_dim(values, start, start + length, axis=along)


def face_divergence(density, velocity, along):
    faces = density.shape[along] - 3
    back_two = window(density, 0, faces, along)
    here = window(density, 1, faces, along)
    ahead = window(density, 2, faces, along)
    ahead_two = window(density, 3, faces, along)
    face_speed = 0.5 * (window(velocity, 1, faces, along) + window(velocity, 2, faces, along))
    flux = jnp.maximum(face_speed, 0.0) * (1.5 * here - 0.5 * back_two) + jnp.minimum(
        face_speed, 0.0
    ) * (1.5 * ahead - 0.5 * ahead_two)
    return window(flux, 1, faces - 1, along) - window(flux, 0, faces - 1, along)


def moved(fluid, step_time):
    density = fluid[0]
    radial = fluid[1]
    azimuth = fluid[2]
    div_azimuth = face_divergence(density, azimuth, 1)
    inner_density = density[:, 2:-2]
    inner_radial = radial[:, 2:-2]
    zero_pad = ((0, 0), (0, 0), (2, 2))
    div_radial = face_divergence(
        jnp.pad(inner_density, zero_pad), jnp.pad(inner_radial, zero_pad), 2
    )
    new_density = inner_density - step_time * (div_azimuth + div_radial)
    gas_density = density[-1]
    inner_gas = gas_density[2:-2]
    grad_azimuth = 0.5 * (gas_density[3:-1] - gas_density[1:-3])
    edge_gas = jnp.pad(inner_gas, ((0, 0), (1, 1)), mode="edge")
    grad_radial = 0.5 * (edge_gas[:, 2:] - edge_gas[:, :-2])
    push = step_time * sound_sq / inner_gas
    gas_velocity = jnp.stack(
        [inner_radial[-1] - push * grad_radial, azimuth[-1, 2:-2] - push * grad_azimuth]
    )
    dust_velocity = jnp.stack([inner_radial[:-1], azimuth[:-1, 2:-2]])
    return (new_density, gas_velocity, dust_velocity)


def drag_terms(new_density, dust_velocity, stop_times, step_time, total_species):
    gas_new = new_density[-1]
    rate = step_time * gas_new[None] / stop_times[:, None, None]
    weight = new_density[:-1] / (total_species * gas_new[None]) * rate / (1.0 + rate)
    terms = jnp.stack(
        [
            jnp.sum(weight, 0),
            jnp.sum(weight * dust_velocity[0], 0),
            jnp.sum(weight * dust_velocity[1], 0),
        ]
    )
    return (rate, terms)


def coupled_gas(gas_velocity, totals):
    return (gas_velocity + totals[1:]) / (1.0 + totals[0])


def assemble(new_density, dust_velocity, gas_next, rate):
    dust_next = (dust_velocity + rate[None] * gas_next[:, None]) / (1.0 + rate[None])
    radial = jnp.concatenate([dust_next[0], gas_next[0][None]], axis=0)
    azimuth = jnp.concatenate([dust_next[1], gas_next[1][None]], axis=0)
    return jnp.stack([new_density, radial, azimuth])


def advance(wide, margin, tile_rows, stop_times, total_species):
    interior = lax.slice_in_dim(wide, margin, margin + tile_rows, axis=2)
    local_top = jnp.max(jnp.abs(interior[1]) + jnp.abs(interior[2]))
    fastest = lax.pmax(local_top, ("space", "species"))
    step_time = courant / (sound_speed + fastest)
    new_density, gas_velocity, dust_velocity = moved(wide, step_time)
    rate, terms = drag_terms(new_density, dust_velocity, stop_times, step_time, total_species)
    totals = lax.psum(terms, "species")
    gas_next = coupled_gas(gas_velocity, totals)
    return assemble(new_density, dust_velocity, gas_next, rate)


def local(dust_state, gas_state, species_bin):
    local_species = dust_state.shape[1]
    total_species = local_species * lax.axis_size("species")
    tile_rows = dust_state.shape[2]
    fluid = jnp.concatenate([dust_state, gas_state[:, None]], axis=1)
    stop_times = stop_floor * jnp.exp(
        stop_span * species_bin.astype(jnp.float32) / (total_species - 1)
    )
    for iteration in range(STEPS):
        wide = padded(fluid, (("space", 2),), 2)
        fluid = advance(wide, 2, tile_rows, stop_times, total_species)
    return (fluid[:, :local_species], fluid[:, local_species])


def solution(mesh):
    placed = (P(None, "species", "space", None), P(None, "space", None), P("species"))
    return jax.shard_map(
        local,
        mesh=mesh,
        in_specs=placed,
        out_specs=(P(None, "species", "space", None), P(None, "space", None)),
        check_vma=False,
    )
```

profile of v0, /device:TPU:4, one launch (start us, length us, event | category | flops | bytes accessed | tf_op | source)
XLA Modules:
  0.0 626.3 jit_solution(17691212085948421090)
XLA Ops:
  7.2 1.4 pad_maximum_fusion.26
  8.7 1.7 collective-permute-start
  11.1 4.1 collective-permute-start.1
  15.2 76.8 %pmax.14 = f32[]{:T(128)} all-reduce(f32[]{:T(128)} %fusion.22), channel_id=1, replica_groups=mesh['space'=8,'species'=32] {'space','species'}, use_global_device_ids=true, to_apply=%region_1.0 | all-reduce | flops 1 | bytes 8 | tf_op jit(solution)/shard_map/pmax | solution.py:98
  96.0 1.2 broadcast_divide_fusion.1
  97.2 1.3 fusion.54
  99.3 1.4 slice_bitcast_fusion.17
  100.9 1.2 fusion.52
  102.1 208.6 %all-reduce.7.cloned.1.call-done = f32[3,32,1024]{2,1,0:T(8,128)} async-done(((f32[3,32,1024]{2,1,0:T(8,128)}), f32[3,32,1024]{2,1,0:T(8,128)}) %all-reduce.7.cloned.1.call-update) | async-done | bytes 393232 | tf_op jit(solution)/shard_map/psum | solution.py:102
  310.7 0.9 fusion.42
  311.6 1.0 fusion.30
  313.0 0.8 add_reduce_fusion
  314.0 1.6 collective-permute-start.2
  315.5 4.2 collective-permute-start.3
  320.5 73.2 %pmax.15 = f32[]{:T(128)} all-reduce(f32[]{:T(128)} %get-tuple-element.30), channel_id=1, replica_groups=mesh['space'=8,'species'=32] {'space','species'}, use_global_device_ids=true, to_apply=%region_7.8 | all-reduce | flops 1 | bytes 8 | tf_op jit(solution)/shard_map/pmax | solution.py:98
  397.1 1.2 broadcast_divide_fusion
  398.3 1.3 fusion.53
  400.3 1.9 fusion.41
  402.3 1.4 fusion.36
  403.7 209.4 %all-reduce.9.cloned.1.call-done = f32[3,32,1024]{2,1,0:T(8,128)} async-done(((f32[3,32,1024]{2,1,0:T(8,128)}), f32[3,32,1024]{2,1,0:T(8,128)}) %all-reduce.9.cloned.1.call-update) | async-done | bytes 393232 | tf_op jit(solution)/shard_map/psum | solution.py:102
  613.1 0.9 fusion.31
  614.0 1.1 fusion.29
  615.1 1.8 fusion.1
  618.3 1.2 copy.7
  (67 shorter events, 10.9 us)
Async XLA Ops:
  7.2 3.2 copy-start
  7.2 3.2 copy-start.1
  7.2 85.5 %copy-start.12 = (s32[4]{0:T(128)S(1)}, s32[4]{0:T(128)}, u32[]{:S(2)}) copy-start(s32[4]{0:T(128)} %param.5) | copy-start | bytes 52
  7.2 303.5 %all-reduce.7.cloned.1.call-start = ((), (), s32[]{:S(2)}) async-start(), calls=%async_computation | async-start | bytes 786432 | tf_op jit(solution)/shard_map/psum | solution.py:102
  8.7 84.0 %collective-permute-start = (f32[3,5,2,1024]{3,2,1,0:T(2,128)S(1)}, f32[3,5,2,1024]{3,2,1,0:T(2,128)S(1)}, u32[]{:S(2)}, u32[]{:S(2)}) collective-permute-start(f32[3,5,2,1024]{3,2,1,0:T(2,128)S(1)} %get-tuple-element.18), channel_id=1, source_target_pairs={{0,32},{32,64},{64,96},{96,128},{128,160},{160,192},{192,224},{224... | collective-permute-start | bytes 368648 | tf_op jit(solution)/shard_map/ppermute | solution.py:20
  11.1 81.6 %collective-permute-start.1 = (f32[3,5,2,1024]{3,2,1,0:T(2,128)S(1)}, f32[3,5,2,1024]{3,2,1,0:T(2,128)S(1)}, u32[]{:S(2)}, u32[]{:S(2)}) collective-permute-start(f32[3,5,2,1024]{3,2,1,0:T(2,128)S(1)} %get-tuple-element.19), channel_id=1, source_target_pairs={{32,0},{64,32},{96,64},{128,96},{160,128},{192,160},{224,192},{0,2... | collective-permute-start | bytes 368648 | tf_op jit(solution)/shard_map/ppermute | solution.py:23
  92.7 0.7 copy-start.10
  92.7 0.7 copy-start.11
  93.4 3.8 copy-start.2
  99.3 513.8 %all-reduce.9.cloned.1.call-start = ((), (), s32[]{:S(2)}) async-start(), calls=%async_computation.1 | async-start | bytes 786432 | tf_op jit(solution)/shard_map/psum | solution.py:102
  100.8 211.9 %copy-start.4 = (f32[4,32,1024]{2,1,0:T(8,128)S(1)}, f32[4,32,1024]{2,1,0:T(8,128)}, u32[]{:S(2)}) copy-start(f32[4,32,1024]{2,1,0:T(8,128)} %get-tuple-element.44) | copy-start | bytes 1572868
  100.8 211.9 %copy-start.5 = (f32[4,32,1024]{2,1,0:T(8,128)S(1)}, f32[4,32,1024]{2,1,0:T(8,128)}, u32[]{:S(2)}) copy-start(f32[4,32,1024]{2,1,0:T(8,128)} %get-tuple-element.46) | copy-start | bytes 1572868
  100.8 211.9 %copy-start.6 = (f32[1,4,32,1024]{3,2,1,0:T(8,128)S(1)}, f32[1,4,32,1024]{3,2,1,0:T(8,128)}, u32[]{:S(2)}) copy-start(f32[1,4,32,1024]{3,2,1,0:T(8,128)} %get-tuple-element.26) | copy-start | bytes 1572868
  100.8 211.9 %copy-start.7 = (f32[1,4,32,1024]{3,2,1,0:T(8,128)S(1)}, f32[1,4,32,1024]{3,2,1,0:T(8,128)}, u32[]{:S(2)}) copy-start(f32[1,4,32,1024]{3,2,1,0:T(8,128)} %get-tuple-element.27) | copy-start | bytes 1572868
  314.0 80.4 %collective-permute-start.2 = (f32[3,5,2,1024]{3,2,1,0:T(2,128)S(1)}, f32[3,5,2,1024]{3,2,1,0:T(2,128)S(1)}, u32[]{:S(2)}, u32[]{:S(2)}) collective-permute-start(f32[3,5,2,1024]{3,2,1,0:T(2,128)S(1)} %get-tuple-element.16), channel_id=1, source_target_pairs={{0,32},{32,64},{64,96},{96,128},{128,160},{160,192},{192,224},{224... | collective-permute-start | bytes 368648 | tf_op jit(solution)/shard_map/ppermute | solution.py:20
  315.5 78.9 %collective-permute-start.3 = (f32[3,5,2,1024]{3,2,1,0:T(2,128)S(1)}, f32[3,5,2,1024]{3,2,1,0:T(2,128)S(1)}, u32[]{:S(2)}, u32[]{:S(2)}) collective-permute-start(f32[3,5,2,1024]{3,2,1,0:T(2,128)S(1)} %get-tuple-element.17), channel_id=1, source_target_pairs={{32,0},{64,32},{96,64},{128,96},{160,128},{192,160},{224,192},{0,2... | collective-permute-start | bytes 368648 | tf_op jit(solution)/shard_map/ppermute | solution.py:23
  394.4 0.7 copy-start.8
  394.4 0.7 copy-start.9
  395.1 3.2 copy-start.3
Sparse Core Ops, SparseCore 0:
  99.4 211.2 all-reduce.6
  400.5 212.5 all-reduce.8
where the time goes:
time: 627 us; the launch traced here: 626 us
  waiting for transfers between devices  418 us (67%)
  blocking collectives  150 us (24%)
  other arithmetic  27 us (4%)
  between operations  15.8 us (3%)
  starting transfers between devices  11.5 us (2%)
    psum x2, waiting for transfers between devices, advance(): totals = lax.psum(terms, 'species')  418 us
    pmax x2, blocking collectives, advance(): fastest = lax.pmax(local_top, ('space', 'species'))  150 us
  transfers between devices with their start and end apart: 6, of which 2 were waited for; matrix products, arithmetic and copies ran while one was open for 1% of the time, Pallas kernels for 0%

commit v1 on v0

--- a/solution.py
+++ b/solution.py
@@ -99,7 +99,8 @@
     step_time = courant / (sound_speed + fastest)
     new_density, gas_velocity, dust_velocity = moved(wide, step_time)
     rate, terms = drag_terms(new_density, dust_velocity, stop_times, step_time, total_species)
-    totals = lax.psum(terms, "species")
+    parts = lax.all_gather(terms, "species", axis=0, tiled=False)
+    totals = parts.sum(axis=0)
     gas_next = coupled_gas(gas_velocity, totals)
     return assemble(new_density, dust_velocity, gas_next, rate)
 

time: 627 us -> 367 us (0.59)
  waiting for transfers between devices: 418 us -> 150 us
    psum x2 -> x0, waiting for transfers between devices: 418 us -> none  [advance(): totals = lax.psum(terms, 'species')]
    all_gather x0 -> x2, waiting for transfers between devices: none -> 150 us  [advance(): parts = lax.all_gather(terms, 'species', axis=0, tiled=False)]
    reduce_sum x0 -> x2, other arithmetic: none -> 11.7 us  [advance(): totals = parts.sum(axis=0)]
  transfers between devices with their start and end apart: 6 -> 6, of which waited for: 2 -> 2; matrix products, arithmetic and copies ran while one was open for 1% -> 2% of each run, Pallas kernels for 0% -> 0%
where the time goes in v1:
time: 367 us; the launch traced here: 365 us
  blocking collectives  150 us (41%)
  waiting for transfers between devices  150 us (41%)
  other arithmetic  33.2 us (9%)
  between operations  15.9 us (4%)
  starting transfers between devices  11.5 us (3%)
  local copies, waits for them, and re-layouts  4.07 us (1%)
    pmax x2, blocking collectives, advance(): fastest = lax.pmax(local_top, ('space', 'species'))  150 us
    all_gather x2, waiting for transfers between devices, advance(): parts = lax.all_gather(terms, 'species', axis=0, tiled=False)  150 us
    reduce_sum x2, other arithmetic, advance(): totals = parts.sum(axis=0)  11.7 us
    ppermute x2, starting transfers between devices, padded(): lax.ppermute(lax.slice_in_dim(block, 0, width, axis=dim), axis, backward)  8.22 us
  transfers between devices with their start and end apart: 6, of which 2 were waited for; matrix products, arithmetic and copies ran while one was open for 2% of the time, Pallas kernels for 0%

profile of v1, /device:TPU:4, one launch (start us, length us, event | category | flops | bytes accessed | tf_op | source)
XLA Modules:
  0.0 364.8 jit_solution(14114853340999102386)
XLA Ops:
  7.2 1.4 pad_maximum_fusion.26
  8.7 1.7 collective-permute-start
  11.1 4.1 %collective-permute-start.1 = (f32[3,5,2,1024]{3,2,1,0:T(2,128)S(1)}, f32[3,5,2,1024]{3,2,1,0:T(2,128)S(1)}, u32[]{:S(2)}, u32[]{:S(2)}) collective-permute-start(f32[3,5,2,1024]{3,2,1,0:T(2,128)S(1)} %get-tuple-element.21), channel_id=1, source_target_pairs={{32,0},{64,32},{96,64},{128,96},{160,128},{192,160},{224,192},{0,2... | collective-permute-start | bytes 368648 | tf_op jit(solution)/shard_map/ppermute | solution.py:23
  15.2 76.8 %pmax.14 = f32[]{:T(128)} all-reduce(f32[]{:T(128)} %fusion.22), channel_id=1, replica_groups=mesh['space'=8,'species'=32] {'space','species'}, use_global_device_ids=true, to_apply=%region_1.0 | all-reduce | flops 1 | bytes 8 | tf_op jit(solution)/shard_map/pmax | solution.py:98
  94.2 0.8 multiply_add_fusion.1
  95.4 1.3 broadcast_divide_fusion.1
  96.6 1.2 fusion.54
  98.7 1.4 slice_bitcast_fusion.17
  100.2 1.7 fusion.52
  101.9 73.8 %all-gather.5.cloned.1.call-done = f32[96,32,1024]{2,1,0:T(8,128)} async-done(((f32[3,32,1024]{2,1,0:T(8,128)}), f32[96,32,1024]{2,1,0:T(8,128)}) %all-gather.5.cloned.1.call-update) | async-done | bytes 12582928 | tf_op jit(solution)/shard_map/all_gather | solution.py:102
  175.7 5.9 %reduce_sum.75 = f32[3,32,1024]{2,1,0:T(8,128)S(1)} reduce(f32[32,3,32,1024]{3,2,1,0:T(8,128)} %bitcast.96, f32[]{:T(128)} %constant.13.clone.1), dimensions={0}, to_apply=%region_5.6 | reduce | flops 3047424 | bytes 12976132 | tf_op jit(solution)/shard_map/reduce_sum | solution.py:103
  181.6 0.9 fusion.30
  183.0 0.8 add_reduce_fusion
  183.9 1.6 collective-permute-start.2
  185.5 4.2 %collective-permute-start.3 = (f32[3,5,2,1024]{3,2,1,0:T(2,128)S(1)}, f32[3,5,2,1024]{3,2,1,0:T(2,128)S(1)}, u32[]{:S(2)}, u32[]{:S(2)}) collective-permute-start(f32[3,5,2,1024]{3,2,1,0:T(2,128)S(1)} %get-tuple-element.19), channel_id=1, source_target_pairs={{32,0},{64,32},{96,64},{128,96},{160,128},{192,160},{224,192},{0,2... | collective-permute-start | bytes 368648 | tf_op jit(solution)/shard_map/ppermute | solution.py:23
  189.6 73.6 %pmax.15 = f32[]{:T(128)} all-reduce(f32[]{:T(128)} %get-tuple-element.32), channel_id=1, replica_groups=mesh['space'=8,'species'=32] {'space','species'}, use_global_device_ids=true, to_apply=%region_7.8 | all-reduce | flops 1 | bytes 8 | tf_op jit(solution)/shard_map/pmax | solution.py:98
  266.0 0.8 multiply_add_fusion
  267.2 1.2 broadcast_divide_fusion
  268.4 1.2 fusion.53
  270.6 1.1 fusion.41
  272.4 75.9 %all-gather.7.cloned.1.call-done = f32[96,32,1024]{2,1,0:T(8,128)} async-done(((f32[3,32,1024]{2,1,0:T(8,128)}), f32[96,32,1024]{2,1,0:T(8,128)}) %all-gather.7.cloned.1.call-update) | async-done | bytes 12582928 | tf_op jit(solution)/shard_map/all_gather | solution.py:102
  348.3 5.9 %reduce_sum.79 = f32[3,32,1024]{2,1,0:T(8,128)S(1)} reduce(f32[32,3,32,1024]{3,2,1,0:T(8,128)} %bitcast.95, f32[]{:T(128)} %constant.13.clone.1), dimensions={0}, to_apply=%region_11.12 | reduce | flops 3047424 | bytes 12976132 | tf_op jit(solution)/shard_map/reduce_sum | solution.py:103
  354.8 0.9 copy-done.4
  356.8 1.2 copy.10
  (85 shorter events, 9.6 us)
Async XLA Ops:
  7.2 3.2 copy-start
  7.2 3.2 copy-start.5
  7.2 85.5 %copy-start.20 = (s32[4]{0:T(128)S(1)}, s32[4]{0:T(128)}, u32[]{:S(2)}) copy-start(s32[4]{0:T(128)} %param.5) | copy-start | bytes 52
  7.2 168.5 %all-gather.5.cloned.1.call-start = ((), (), s32[]{:S(2)}) async-start(), calls=%async_computation | async-start | bytes 12976128 | tf_op jit(solution)/shard_map/all_gather | solution.py:102
  8.7 84.0 %collective-permute-start = (f32[3,5,2,1024]{3,2,1,0:T(2,128)S(1)}, f32[3,5,2,1024]{3,2,1,0:T(2,128)S(1)}, u32[]{:S(2)}, u32[]{:S(2)}) collective-permute-start(f32[3,5,2,1024]{3,2,1,0:T(2,128)S(1)} %get-tuple-element.20), channel_id=1, source_target_pairs={{0,32},{32,64},{64,96},{96,128},{128,160},{160,192},{192,224},{224... | collective-permute-start | bytes 368648 | tf_op jit(solution)/shard_map/ppermute | solution.py:20
  11.1 81.6 %collective-permute-start.1 = (f32[3,5,2,1024]{3,2,1,0:T(2,128)S(1)}, f32[3,5,2,1024]{3,2,1,0:T(2,128)S(1)}, u32[]{:S(2)}, u32[]{:S(2)}) collective-permute-start(f32[3,5,2,1024]{3,2,1,0:T(2,128)S(1)} %get-tuple-element.21), channel_id=1, source_target_pairs={{32,0},{64,32},{96,64},{128,96},{160,128},{192,160},{224,192},{0,2... | collective-permute-start | bytes 368648 | tf_op jit(solution)/shard_map/ppermute | solution.py:23
  93.4 3.3 copy-start.6
  98.6 249.7 %all-gather.7.cloned.1.call-start = ((), (), s32[]{:S(2)}) async-start(), calls=%async_computation.1 | async-start | bytes 12976128 | tf_op jit(solution)/shard_map/all_gather | solution.py:102
  175.7 5.9 %copy-start.16 = (f32[1,32,1024]{2,1,0:T(8,128)S(1)}, f32[1,32,1024]{2,1,0:T(8,128)}, u32[]{:S(2)}) copy-start(f32[1,32,1024]{2,1,0:T(8,128)} %get-tuple-element.38) | copy-start | bytes 393220
  175.7 6.9 %copy-start.10 = (f32[4,32,1024]{2,1,0:T(8,128)S(1)}, f32[4,32,1024]{2,1,0:T(8,128)}, u32[]{:S(2)}) copy-start(f32[4,32,1024]{2,1,0:T(8,128)} %get-tuple-element.46) | copy-start | bytes 1572868
  175.7 6.9 %copy-start.11 = (f32[4,32,1024]{2,1,0:T(8,128)S(1)}, f32[4,32,1024]{2,1,0:T(8,128)}, u32[]{:S(2)}) copy-start(f32[4,32,1024]{2,1,0:T(8,128)} %get-tuple-element.48) | copy-start | bytes 1572868
  175.7 6.9 %copy-start.12 = (f32[1,4,32,1024]{3,2,1,0:T(8,128)S(1)}, f32[1,4,32,1024]{3,2,1,0:T(8,128)}, u32[]{:S(2)}) copy-start(f32[1,4,32,1024]{3,2,1,0:T(8,128)} %get-tuple-element.28) | copy-start | bytes 1572868
  175.7 6.9 %copy-start.13 = (f32[1,4,32,1024]{3,2,1,0:T(8,128)S(1)}, f32[1,4,32,1024]{3,2,1,0:T(8,128)}, u32[]{:S(2)}) copy-start(f32[1,4,32,1024]{3,2,1,0:T(8,128)} %get-tuple-element.29) | copy-start | bytes 1572868
  183.8 80.1 %copy-start.1 = (f32[1,5,32,1024]{3,2,1,0:T(8,128)}, f32[1,5,32,1024]{3,2,1,0:T(8,128)S(1)}, u32[]{:S(2)}) copy-start(f32[1,5,32,1024]{3,2,1,0:T(8,128)S(1)} %get-tuple-element.34) | copy-start | bytes 1966084
  183.9 80.0 %collective-permute-start.2 = (f32[3,5,2,1024]{3,2,1,0:T(2,128)S(1)}, f32[3,5,2,1024]{3,2,1,0:T(2,128)S(1)}, u32[]{:S(2)}, u32[]{:S(2)}) collective-permute-start(f32[3,5,2,1024]{3,2,1,0:T(2,128)S(1)} %get-tuple-element.18), channel_id=1, source_target_pairs={{0,32},{32,64},{64,96},{96,128},{128,160},{160,192},{192,224},{224... | collective-permute-start | bytes 368648 | tf_op jit(solution)/shard_map/ppermute | solution.py:20
  185.5 78.5 %collective-permute-start.3 = (f32[3,5,2,1024]{3,2,1,0:T(2,128)S(1)}, f32[3,5,2,1024]{3,2,1,0:T(2,128)S(1)}, u32[]{:S(2)}, u32[]{:S(2)}) collective-permute-start(f32[3,5,2,1024]{3,2,1,0:T(2,128)S(1)} %get-tuple-element.19), channel_id=1, source_target_pairs={{32,0},{64,32},{96,64},{128,96},{160,128},{192,160},{224,192},{0,2... | collective-permute-start | bytes 368648 | tf_op jit(solution)/shard_map/ppermute | solution.py:23
  265.2 3.2 copy-start.7
  267.2 2.5 copy-start.3
  268.4 3.2 copy-start.2
  348.3 6.0 %copy-start.8 = (f32[4,32,1024]{2,1,0:T(8,128)S(1)}, f32[4,32,1024]{2,1,0:T(8,128)}, u32[]{:S(2)}) copy-start(f32[4,32,1024]{2,1,0:T(8,128)} %get-tuple-element.43) | copy-start | bytes 1572868
  348.3 6.0 %copy-start.9 = (f32[4,32,1024]{2,1,0:T(8,128)S(1)}, f32[4,32,1024]{2,1,0:T(8,128)}, u32[]{:S(2)}) copy-start(f32[4,32,1024]{2,1,0:T(8,128)} %get-tuple-element.45) | copy-start | bytes 1572868
  348.3 6.0 %copy-start.14 = (f32[1,4,32,1024]{3,2,1,0:T(8,128)S(1)}, f32[1,4,32,1024]{3,2,1,0:T(8,128)}, u32[]{:S(2)}) copy-start(f32[1,4,32,1024]{3,2,1,0:T(8,128)} %get-tuple-element.26) | copy-start | bytes 1572868
  348.3 6.0 %copy-start.15 = (f32[1,4,32,1024]{3,2,1,0:T(8,128)S(1)}, f32[1,4,32,1024]{3,2,1,0:T(8,128)}, u32[]{:S(2)}) copy-start(f32[1,4,32,1024]{3,2,1,0:T(8,128)} %get-tuple-element.27) | copy-start | bytes 1572868
  354.6 1.1 copy-start.4
  (3 other events, 2.0 us)
Sparse Core Ops, SparseCore 0:
  98.8 76.9 all-gather.4
  270.6 77.6 all-gather.6
